TPU v7x, 32 devices: a whole 2x2x4 slice. The times are simulated.
32 devices in a mesh: groups: 2 (over y), blk: 4 (over z), cls: 4 (over x, core).
Axes of the slice: x: 2, y: 2, z: 4, core: 2. Of those that a mesh axis runs over, the one named last changes fastest.
Arguments:
- particles: bfloat16 [64, 4096], P(('groups', 'blk')), parts along dimension 0
- references: bfloat16 [4, 400, 4096], P('blk', ('groups', 'cls')), parts along dimension 1
- ctf_table: float32 [32, 2048], P('groups'), parts along dimension 0, may hold values from 0.05 to 1
- spectral_reg: float32 [4096], P('groups'), parts along dimension 0, may hold values from 0.002 to 0.02
- defocus_bin: int32 [64], P(('groups', 'blk')), parts along dimension 0, may hold values from 0 to 15
- group_counts: int32 [32], P(('groups', 'blk')), parts along dimension 0, may hold values from 0 to 8, as said below
- group_scale: float32 [32], P(('groups', 'blk')), parts along dimension 0, may hold values from 0.5 to 2
Outputs:
- class_average: float32 [4, 400, 4096], P('blk', ('groups', 'cls')), parts along dimension 1
- log_evidence: float32 [64], P(('groups', 'blk')), parts along dimension 0
There are 2 independent parts, one for each index of `groups`. A program takes and returns all parts, laid end to end along the dimension named above; each array names one. Nothing has to cross between parts.
Inputs may be any that keep to these rules, and one draw needn't show every extreme that they name: `group_counts`: the 4 groups of one block of 8 slots hold at most 8 particles together, filling the block's first slots; in every draw some single group holds exactly 8.
All inputs are finite; a program needn't handle non-finite values.
Results may differ from a plain program's by a relative error of at most 0.013.
Values may be sent and summed in bfloat16 or wider, within the bound.
No kernel may reach another device: no remote copies, remote signals or barrier semaphores. Data moves between devices by JAX's collectives and lax.ppermute only.
A program may use at most 64 MiB of HBM per device.

v0:
```python
import math
import jax
import jax.numpy as jnp
from jax import lax
from jax.sharding import PartitionSpec as P

KX = 32
KY = 64
IMG = 128
SIDE = 4
BINS = 16
HIGHEST = lax.Precision.HIGHEST


def combined_all(value, axis, join):
    pieces = jax.tree.map(lambda part: lax.all_gather(part, axis), value)
    head = jax.tree.map(lambda part: part[0], pieces)
    tail = jax.tree.map(lambda part: part[1:], pieces)
    running, _ = lax.scan(lambda running, section: (join(running, section), None), head, tail)
    return running


def phase_tables():
    column = jnp.arange(KX * KY, dtype=jnp.int32)
    freq_x = (column % KX).astype(jnp.float32)
    freq_y = (column // KX - KY // 2).astype(jnp.float32)
    offsets = jnp.arange(SIDE, dtype=jnp.float32) - (SIDE - 1) / 2.0
    shift_x = jnp.tile(offsets, SIDE)
    shift_y = jnp.repeat(offsets, SIDE)
    phases = (
        2.0
        * math.pi
        / IMG
        * (shift_x[:, None] * freq_x[None, :] + shift_y[:, None] * freq_y[None, :])
    )
    return (jnp.cos(phases), jnp.sin(phases))


def bin_matrix(bin_values):
    return (bin_values[:, None] == jnp.arange(BINS, dtype=jnp.float32)[None, :]).astype(jnp.float32)


def slot_weights(group_sizes, scale_rows, slots):
    group_ends = jnp.cumsum(group_sizes, axis=1)
    group_starts = group_ends - group_sizes
    slot_index = jnp.arange(slots, dtype=jnp.int32)
    membership = (
        (slot_index[None, :, None] >= group_starts[:, None, :])
        & (slot_index[None, :, None] < group_ends[:, None, :])
    ).astype(jnp.float32)
    gain_rows = jnp.sum(membership * scale_rows[:, None, :], axis=2)
    live_mask = jnp.sum(membership, axis=2)
    return (gain_rows.reshape(-1), live_mask.reshape(-1))


def shifted_rows(images, ctf_rows, cosine_table, sine_table):
    half_width = ctf_rows.shape[1]
    real_part = images[:, :half_width].astype(jnp.float32)[:, None, :]
    imag_part = images[:, half_width:].astype(jnp.float32)[:, None, :]
    ctf_wide = ctf_rows[:, None, :]
    new_real = (real_part * cosine_table + imag_part * sine_table) * ctf_wide
    new_imag = (imag_part * cosine_table - real_part * sine_table) * ctf_wide
    joined = jnp.concatenate([new_real, new_imag], axis=2).astype(jnp.bfloat16)
    return joined.reshape(images.shape[0] * cosine_table.shape[0], 2 * half_width)


def tile_norms(ref_rows, ctf_square):
    half_width = ctf_square.shape[1]
    values = ref_rows.astype(jnp.float32)
    power_sum = (
        values[:, :half_width] * values[:, :half_width]
        + values[:, half_width:] * values[:, half_width:]
    )
    return lax.dot_general(ctf_square, power_sum, (((1,), (1,)), ((), ())), precision=HIGHEST)


def tile_scores(shifted, ref_rows, norms, gain_rows, bin_rows):
    count_here = gain_rows.shape[0]
    products = lax.dot_general(
        shifted, ref_rows, (((1,), (1,)), ((), ())), preferred_element_type=jnp.float32
    )
    products = products.reshape(count_here, shifted.shape[0] // count_here, ref_rows.shape[0])
    norm_term = jnp.dot(bin_rows, norms, precision=HIGHEST)
    return (
        gain_rows[:, None, None] * products
        - 0.5 * (gain_rows * gain_rows)[:, None, None] * norm_term[:, None, :]
    )


def combine_stats(former, latter):
    new_peak = jnp.maximum(former[0], latter[0])
    return (
        new_peak,
        former[1] * jnp.exp(former[0] - new_peak) + latter[1] * jnp.exp(latter[0] - new_peak),
    )


def accumulate(running, shifted, scores, gain_rows, bin_rows, live_mask, peak_score, totals):
    weights = (
        jnp.exp(scores - peak_score[:, None, None])
        / totals[:, None, None]
        * live_mask[:, None, None]
    )
    scaled = (weights * gain_rows[:, None, None]).astype(jnp.bfloat16).reshape(shifted.shape[0], -1)
    numerator = running[0] + lax.dot_general(
        scaled, shifted, (((0,), (0,)), ((), ())), preferred_element_type=jnp.float32
    )
    summed = jnp.sum(weights, axis=1) * (gain_rows * gain_rows)[:, None]
    bin_weight = running[1] + lax.dot_general(
        summed, bin_rows, (((0,), (0,)), ((), ())), precision=HIGHEST
    )
    return (numerator, bin_weight)


def per_device(
    particles, references, ctf_table, spectral_reg, defocus_bin, group_counts, group_scale
):
    cosine_table, sine_table = phase_tables()
    ctf_square = ctf_table * ctf_table
    batch_size = particles.shape[0]
    gain_rows, live_mask = slot_weights(
        group_counts.reshape(1, -1), group_scale.reshape(1, -1), batch_size
    )
    bin_values = defocus_bin.astype(jnp.float32)
    ref_tile = references[0]
    own_norms = tile_norms(ref_tile, ctf_square)
    classes_here = ref_tile.shape[0]
    zero_sums = (
        jnp.zeros((classes_here, ref_tile.shape[1]), jnp.float32),
        jnp.zeros((classes_here, ctf_table.shape[0]), jnp.float32),
    )

    def batch_rows(images, bins_part):
        bin_rows = bin_matrix(bins_part)
        ctf_rows = jnp.dot(bin_rows, ctf_table, precision=HIGHEST)
        return (shifted_rows(images, ctf_rows, cosine_table, sine_table), bin_rows)

    everyone = lax.all_gather(particles, "blk", axis=0, tiled=True)
    gain_all, bins_all, live_all = (
        lax.all_gather(gain_rows, "blk", axis=0, tiled=True),
        lax.all_gather(bin_values, "blk", axis=0, tiled=True),
        lax.all_gather(live_mask, "blk", axis=0, tiled=True),
    )
    whole_count = everyone.shape[0]
    block_size = math.gcd(whole_count, 32)
    block_count = whole_count // block_size

    def block_inputs(block_index):
        offset = block_index * block_size
        images = lax.dynamic_slice_in_dim(everyone, offset, block_size)
        gains_part = lax.dynamic_slice_in_dim(gain_all, offset, block_size)
        shifted, bin_rows = batch_rows(
            images, lax.dynamic_slice_in_dim(bins_all, offset, block_size)
        )
        return (offset, shifted, bin_rows, gains_part)

    def block_scores(block_index):
        offset, shifted, bin_rows, gains_part = block_inputs(block_index)
        return tile_scores(shifted, ref_tile, own_norms, gains_part, bin_rows)

    all_scores = lax.map(block_scores, jnp.arange(block_count, dtype=jnp.int32))
    all_scores = all_scores.reshape(whole_count, cosine_table.shape[0], classes_here)
    flattened = all_scores.reshape(whole_count, -1)
    peak_all = jnp.max(flattened, axis=1)
    totals_all = jnp.sum(jnp.exp(flattened - peak_all[:, None]), axis=1)
    peak_all, totals_all = combined_all((peak_all, totals_all), ("blk", "cls"), combine_stats)

    def block_sums(block_index, running):
        offset, shifted, bin_rows, gains_part = block_inputs(block_index)
        scores = lax.dynamic_slice_in_dim(all_scores, offset, block_size)
        live_part = lax.dynamic_slice_in_dim(live_all, offset, block_size)
        peak_part = lax.dynamic_slice_in_dim(peak_all, offset, block_size)
        totals_part = lax.dynamic_slice_in_dim(totals_all, offset, block_size)
        return accumulate(
            running, shifted, scores, gains_part, bin_rows, live_part, peak_part, totals_part
        )

    numerator, bin_weight = lax.fori_loop(0, block_count, block_sums, zero_sums)
    own_offset = lax.axis_index("blk") * batch_size
    peak_score = lax.dynamic_slice_in_dim(peak_all, own_offset, batch_size)
    totals = lax.dynamic_slice_in_dim(totals_all, own_offset, batch_size)
    log_evidence = jnp.where(live_mask > 0.5, peak_score + jnp.log(totals), 0.0)
    denominator = jnp.dot(bin_weight, ctf_square, precision=HIGHEST)
    denominator = (
        jnp.concatenate([denominator, denominator], axis=1)
        + jnp.concatenate([spectral_reg, spectral_reg])[None, :]
    )
    class_average = (numerator / denominator)[None]
    return (class_average, log_evidence)


def solution(mesh):
    placed = (
        P(("groups", "blk"), None),
        P("blk", ("groups", "cls"), None),
        P("groups", None),
        P("groups"),
        P(("groups", "blk")),
        P(("groups", "blk")),
        P(("groups", "blk")),
    )
    return jax.shard_map(
        per_device,
        mesh=mesh,
        in_specs=placed,
        out_specs=(P("blk", ("groups", "cls"), None), P(("groups", "blk"))),
        check_vma=False,
    )
```

profile of v0, /device:TPU:0, one launch (start us, length us, event | category | flops | bytes accessed | tf_op | source)
XLA Modules:
  0.0 79.3 jit_solution(13035143194727210498)
XLA Ops:
  0.6 0.0 copy-start.1
  0.6 0.0 copy-start.2
  0.7 1.3 %dynamic-slice.2 = u32[1]{0:T(128)} dynamic-slice(u32[32]{0:T(128)} %constant.106, u32[]{:T(128)S(6)} %add.107), dynamic_slice_sizes={1} | dynamic-slice | bytes 12
  2.6 1.2 %dynamic-slice = u32[1]{0:T(128)} dynamic-slice(u32[32]{0:T(128)} %constant.96, u32[]{:T(128)S(6)} %add.107), dynamic_slice_sizes={1} | dynamic-slice | bytes 12
  4.5 0.8 %reduce-window.7 = s32[4,1]{0,1:T(1,128)S(1)} reduce-window(s32[4,1]{0,1:T(1,128)} %bitcast.39, s32[]{:T(128)} %copy.31), window={size=4x1 pad=3_0x0_0}, to_apply=%region_0.1 | reduce-window | flops 12 | bytes 36 | tf_op jit(solution)/shard_map/reduce-window.2
  5.3 0.7 bitcast_subtract_fusion
  6.0 0.7 select_reduce_fusion
  6.7 0.2 dynamic-update-slice.4
  7.0 0.7 convert_dynamic-update-slice_fusion
  7.7 0.2 dynamic-update-slice
  7.9 13.4 %all-reduce.6 = (f32[32]{0:T(128)S(1)}, f32[32]{0:T(128)S(1)}, f32[32]{0:T(128)S(1)}) all-reduce(f32[32]{0:T(128)S(1)} %convert_dynamic-update-slice_fusion, f32[32]{0:T(128)S(1)} %dynamic-update-slice.4, f32[32]{0:T(128)S(1)} %dynamic-update-slice), channel_id=1, replica_groups=mesh['groups'=2,'blk'=4,'cls'=4] {'blk'}, use_global_device_ids=true, to_apply=%add.1 | all-reduce | flops 96 | bytes 768
  21.4 0.1 broadcast_in_dim.50
  21.4 0.1 mul.359
  21.5 0.1 mul.355
  21.6 0.8 pad_maximum_fusion.7
  22.4 0.5 fusion.15
  22.9 1.2 %fusion.22 = f32[32,2048]{1,0:T(8,128)S(1)} fusion(f32[16,2048]{1,0:T(8,128)} %param.11, f32[32]{0:T(128)S(1)} %get-tuple-element.122), kind=kOutput, calls=%fused_computation.40 | convolution fusion | flops 12583424 | bytes 393344 | tf_op jit(solution)/shard_map/while/body/eval_jaxpr/dot_general | solution.py:135
  24.2 14.1 %all_gather.25 = bf16[32,4096]{1,0:T(8,128)(2,1)S(1)} all-gather(bf16[8,4096]{1,0:T(8,128)(2,1)} %param.9), channel_id=1, replica_groups=mesh['groups'=2,'blk'=4,'cls'=4] {'blk'}, dimensions={0}, use_global_device_ids=true | all-gather | bytes 327680 | tf_op jit(solution)/shard_map/all_gather | solution.py:138
  38.3 0.0 copy-done.2
  38.3 0.1 bitcast_convert_fusion
  38.4 0.0 copy-done.1
  38.4 0.5 fusion.11
  38.8 0.2 convolution_multiply_fusion
  39.1 1.5 %multiply_convert_fusion.1 = (bf16[32,16,2048]{2,1,0:T(8,128)(2,1)S(1)}, bf16[32,16,2048]{2,1,0:T(8,128)(2,1)S(1)}) fusion(f32[32,2048]{1,0:T(8,128)S(1)} %fusion.22, f32[16,2048]{1,0:T(8,128)S(1)} %get-tuple-element.132, f32[32,2048]{1,0:T(8,128)S(1)} %get-tuple-element.130, f32[16,2048]{1,0:T(8,128)S(1)} %get-tuple-element.131, ...), kind=kLoop, calls=%fused_computation.12 | loop fusion | flops 10485760 | bytes 5242880 | tf_op jit(solution)/shard_map/convert
  40.6 0.0 copy-start
  40.6 1.4 %fusion.40 = (f32[32]{0:T(128)S(1)}, f32[32,16,50]{2,1,0:T(8,128)S(1)}) fusion(f32[32,50]{1,0:T(8,128)S(1)} %convolution_multiply_fusion, bf16[1,50,4096]{2,1,0:T(8,128)(2,1)S(1)} %copy-done.2, bf16[32,16,2048]{2,1,0:T(8,128)(2,1)S(1)} %get-tuple-element.128, bf16[32,16,2048]{2,1,0:T(8,128)(2,1)S(1)} %get-tuple-element.127, f32[32]{0:T(128)S(1)} %get-tuple-element.124), kind=kOutput, calls=%fused_computation.71 | convolution fusion | flops 218180576 | bytes 4712960 | tf_op jit(solution)/shard_map/while/body/eval_jaxpr/dot_general | solution.py:79
  42.1 0.0 copy-done
  42.1 0.2 dynamic-update-slice.2
  42.3 0.5 exponential_reduce_fusion
  42.8 0.2 dynamic-update-slice.3
  43.0 29.5 %all-reduce.5 = (f32[512]{0:T(512)S(1)}, f32[512]{0:T(512)S(1)}) all-reduce(f32[512]{0:T(512)S(1)} %dynamic-update-slice.2, f32[512]{0:T(512)S(1)} %dynamic-update-slice.3), channel_id=2, replica_groups=mesh['groups'=2,'blk'=4,'cls'=4] {'blk','cls'}, use_global_device_ids=true, to_apply=%add.2 | all-reduce | flops 1024 | bytes 8192
  72.5 0.1 slice.42
  72.6 0.1 slice.43
  72.7 0.1 reshape.391
  72.7 0.1 reshape.390
  72.8 0.6 while.2
  73.4 0.6 compare_select_fusion
  74.0 0.2 fusion.38
  74.2 0.3 fusion.20
  74.5 0.5 fusion.17
  75.0 2.6 %fusion.6 = f32[1,50,4096]{2,1,0:T(8,128)S(1)} fusion(bf16[32,16,2048]{2,1,0:T(8,128)(2,1)} %copy-done, bf16[32,16,2048]{2,1,0:T(8,128)(2,1)S(1)} %get-tuple-element.127, f32[50,2048]{1,0:T(8,128)S(1)} %fusion.17, f32[4096]{0:T(1024)S(1)} %pad_maximum_fusion.7, f32[32]{0:T(128)S(1)} %get-tuple-element.124, f32[32,16,50]{2,1,0:T(8,128)S(1)} %get-tuple-element.136, ...), kind=kOutput, calls=%fused_computation.9 | convolution fusion | flops 218846208 | bytes 5542400 | tf_op jit(solution)/shard_map/while/body/eval_jaxpr/dot_general | solution.py:105
  77.6 1.7 %copy.14 = f32[1,50,4096]{2,0,1:T(1,128)} copy(f32[1,50,4096]{2,1,0:T(8,128)S(1)} %fusion.6) | data formatting | bytes 1638400
  (27 shorter events, 0.5 us)
Async XLA Ops:
  0.6 37.7 %copy-start.1 = (f32[16,2048]{1,0:T(8,128)S(1)}, f32[16,2048]{1,0:T(8,128)}, u32[]{:S(2)}) copy-start(f32[16,2048]{1,0:T(8,128)} %param.11) | copy-start | bytes 393220
  0.6 37.6 %copy-start.2 = (bf16[1,50,4096]{2,1,0:T(8,128)(2,1)S(1)}, bf16[1,50,4096]{2,1,0:T(8,128)(2,1)}, u32[]{:S(2)}) copy-start(bf16[1,50,4096]{2,1,0:T(8,128)(2,1)} %param.10) | copy-start | bytes 1228804
  40.6 1.5 %copy-start = (bf16[32,16,2048]{2,1,0:T(8,128)(2,1)}, bf16[32,16,2048]{2,1,0:T(8,128)(2,1)S(1)}, u32[]{:S(2)}) copy-start(bf16[32,16,2048]{2,1,0:T(8,128)(2,1)S(1)} %get-tuple-element.128) | copy-start | bytes 6291460
where the time goes:
time: 79.7 us; the launch traced here: 79.3 us
  blocking collectives  57 us (72%)
  other arithmetic  7.63 us (10%)
  matrix products  6.69 us (8%)
  local copies, waits for them, and re-layouts  5.77 us (7%)
  between operations  2.08 us (3%)
    unnamed x2, blocking collectives  42.9 us
    all_gather x1, blocking collectives, per_device(): everyone = lax.all_gather(particles, 'blk', axis=0, tiled=True)  14.1 us
    unnamed x18, local copies, waits for them, and re-layouts  5.22 us
    dot_general x1, matrix products, accumulate(): lax.dot_general(scaled, shifted, (((0,), (0,)), ((), ())), preferred_elem...  2.57 us
    another operation x2, other arithmetic  2.37 us

commit v1 on v0

--- a/solution.py
+++ b/solution.py
@@ -135,7 +135,12 @@
         ctf_rows = jnp.dot(bin_rows, ctf_table, precision=HIGHEST)
         return (shifted_rows(images, ctf_rows, cosine_table, sine_table), bin_rows)
 
-    everyone = lax.all_gather(particles, "blk", axis=0, tiled=True)
+    ring = [particles]
+    for hop in range(3):
+        ring.append(lax.ppermute(ring[-1], "blk", [(dev, (dev + 1) % 4) for dev in range(4)]))
+    everyone = jnp.roll(
+        jnp.concatenate(ring[::-1], axis=0), (lax.axis_index("blk") + 1) * ring[0].shape[0], axis=0
+    )
     gain_all, bins_all, live_all = (
         lax.all_gather(gain_rows, "blk", axis=0, tiled=True),
         lax.all_gather(bin_values, "blk", axis=0, tiled=True),

time: 79.7 us -> 76.9 us (0.965)
  blocking collectives: 57 us -> 39.9 us
  waiting for transfers between devices: 0 us -> 10.5 us
  starting transfers between devices: 0 us -> 3.28 us
  matrix products: 6.69 us -> 7.56 us
    all_gather x1 -> x0, blocking collectives: 14.1 us -> none  [per_device(): everyone = lax.all_gather(particles, 'blk', axis=0, tiled=True)]
    ppermute x0 -> x3, waiting for transfers between devices: none -> 10.5 us  [per_device(): lax.ppermute(ring[-1], 'blk', [(dev, (dev + 1) % 4) for dev in range(4)])]
    ppermute x0 -> x3, starting transfers between devices: none -> 3.28 us  [per_device(): lax.ppermute(ring[-1], 'blk', [(dev, (dev + 1) % 4) for dev in range(4)])]
    unnamed x2, blocking collectives: 42.9 us -> 39.9 us
    convert_element_type x1, other arithmetic: 0.06 us -> 1.08 us  [tile_norms(): values = ref_rows.astype(jnp.float32)]
    dot_general x1, matrix products: 0.48 us -> 1.38 us  [tile_norms(): lax.dot_general(ctf_square, power_sum, (((1,), (1,)), ((), ())), precisio...]
    unnamed x18 -> x31, local copies, waits for them, and re-layouts: 5.22 us -> 4.54 us
  transfers between devices with their start and end apart: 0 -> 3, of which waited for: 0 -> 2; matrix products, arithmetic and copies ran while one was open for 0% -> 13% of each run, Pallas kernels for 0% -> 0%
where the time goes in v1:
time: 76.9 us; the launch traced here: 76.6 us
  blocking collectives  39.9 us (52%)
  waiting for transfers between devices  10.5 us (14%)
  other arithmetic  7.88 us (10%)
  matrix products  7.56 us (10%)
  local copies, waits for them, and re-layouts  5.09 us (7%)
  starting transfers between devices  3.28 us (4%)
  between operations  2.21 us (3%)
    unnamed x2, blocking collectives  39.9 us
    ppermute x3, waiting for transfers between devices, per_device(): lax.ppermute(ring[-1], 'blk', [(dev, (dev + 1) % 4) for dev in range(4)])  10.5 us
    unnamed x31, local copies, waits for them, and re-layouts  4.54 us
    ppermute x3, starting transfers between devices, per_device(): lax.ppermute(ring[-1], 'blk', [(dev, (dev + 1) % 4) for dev in range(4)])  3.28 us
    dot_general x1, matrix products, accumulate(): lax.dot_general(scaled, shifted, (((0,), (0,)), ((), ())), preferred_elem...  2.57 us
    another operation x2, other arithmetic  2.36 us
  transfers between devices with their start and end apart: 3, of which 2 were waited for; matrix products, arithmetic and copies ran while one was open for 13% of the time, Pallas kernels for 0%

profile of v1, /device:TPU:0, one launch (start us, length us, event | category | flops | bytes accessed | tf_op | source)
XLA Modules:
  0.0 76.6 jit_solution(4754930952773371339)
XLA Ops:
  0.6 0.0 copy-start.5
  0.6 0.0 copy-start.3
  0.7 3.1 %collective-permute-start = (bf16[8,4096]{1,0:T(8,128)(2,1)}, bf16[8,4096]{1,0:T(8,128)(2,1)S(1)}, u32[]{:S(2)}, u32[]{:S(2)}) collective-permute-start(bf16[8,4096]{1,0:T(8,128)(2,1)} %param.9), channel_id=1, source_target_pairs={{0,4},{4,8},{8,12},{12,0},{1,5},{5,9},{9,13},{13,1},{2,6},{6,10},{... | collective-permute-start | bytes 196616 | tf_op jit(solution)/shard_map/ppermute | solution.py:140
  3.8 0.8 %reduce-window.7 = s32[4,1]{0,1:T(1,128)S(1)} reduce-window(s32[4,1]{0,1:T(1,128)} %bitcast.39, s32[]{:T(128)} %copy.38), window={size=4x1 pad=3_0x0_0}, to_apply=%region_0.1 | reduce-window | flops 12 | bytes 36 | tf_op jit(solution)/shard_map/reduce-window.2
  4.6 0.7 bitcast_subtract_fusion
  5.2 0.1 broadcast_in_dim.50
  5.3 0.1 mul.363
  5.4 0.1 mul.359
  5.5 1.1 %bitcast_convert_fusion = f32[50,4096]{1,0:T(8,128)S(1)} fusion(bf16[1,50,4096]{2,1,0:T(8,128)(2,1)} %param.10), kind=kLoop, calls=%fused_computation.23 | loop fusion | flops 204800 | bytes 1228800 | tf_op jit(solution)/shard_map/convert_element_type | solution.py:69
  6.6 1.2 %dynamic-slice = u32[1]{0:T(128)} dynamic-slice(u32[32]{0:T(128)} %constant.113, u32[]{:T(128)S(6)} %add.123), dynamic_slice_sizes={1} | dynamic-slice | bytes 12
  8.5 0.7 select_reduce_fusion
  9.2 0.2 dynamic-update-slice.4
  9.5 0.7 convert_dynamic-update-slice_fusion
  10.2 0.2 dynamic-update-slice
  10.4 10.4 %all-reduce.6 = (f32[32]{0:T(128)S(1)}, f32[32]{0:T(128)S(1)}, f32[32]{0:T(128)S(1)}) all-reduce(f32[32]{0:T(128)S(1)} %convert_dynamic-update-slice_fusion, f32[32]{0:T(128)S(1)} %dynamic-update-slice.4, f32[32]{0:T(128)S(1)} %dynamic-update-slice), channel_id=1, replica_groups=mesh['groups'=2,'blk'=4,'cls'=4] {'blk'}, use_global_device_ids=true, to_apply=%add.1 | all-reduce | flops 96 | bytes 768
  20.8 1.2 %fusion.22 = f32[32,2048]{1,0:T(8,128)S(1)} fusion(f32[16,2048]{1,0:T(8,128)} %param.11, f32[32]{0:T(128)S(1)} %get-tuple-element.122), kind=kOutput, calls=%fused_computation.48 | convolution fusion | flops 12583424 | bytes 393344 | tf_op jit(solution)/shard_map/while/body/eval_jaxpr/dot_general | solution.py:135
  22.0 1.4 %fusion.11 = f32[16,50]{1,0:T(8,128)S(1)} fusion(f32[50,4096]{1,0:T(8,128)S(1)} %bitcast_convert_fusion, f32[16,2048]{1,0:T(8,128)} %param.11), kind=kOutput, calls=%fused_computation.20 | convolution fusion | flops 20000768 | bytes 953472 | tf_op jit(solution)/shard_map/dot_general | solution.py:74
  23.4 0.6 fusion.15
  24.0 0.0 collective-permute-done
  24.0 0.2 collective-permute-start.1
  24.2 0.2 convolution_multiply_fusion
  24.4 0.6 dynamic-slice.2
  25.6 4.4 %collective-permute-done.1 = bf16[8,4096]{1,0:T(8,128)(2,1)S(1)} collective-permute-done((bf16[8,4096]{1,0:T(8,128)(2,1)S(1)}, bf16[8,4096]{1,0:T(8,128)(2,1)S(1)}, u32[]{:S(2)}, u32[]{:S(2)}) %collective-permute-start.1) | collective-permute-done | bytes 65568 | tf_op jit(solution)/shard_map/ppermute | solution.py:140
  30.1 0.0 collective-permute-start.2
  30.1 6.1 %collective-permute-done.2 = bf16[8,4096]{1,0:T(8,128)(2,1)S(1)} collective-permute-done((bf16[8,4096]{1,0:T(8,128)(2,1)S(1)}, bf16[8,4096]{1,0:T(8,128)(2,1)S(1)}, u32[]{:S(2)}, u32[]{:S(2)}) %collective-permute-start.2) | collective-permute-done | bytes 65568 | tf_op jit(solution)/shard_map/ppermute | solution.py:140
  36.2 0.0 copy-done.3
  36.3 0.0 copy-start.2
  36.3 1.5 %multiply_convert_fusion.1 = (bf16[32,16,2048]{2,1,0:T(8,128)(2,1)S(1)}, bf16[32,16,2048]{2,1,0:T(8,128)(2,1)S(1)}) fusion(f32[32,2048]{1,0:T(8,128)S(1)} %fusion.22, f32[16,2048]{1,0:T(8,128)S(1)} %get-tuple-element.132, f32[32,2048]{1,0:T(8,128)S(1)} %get-tuple-element.130, f32[16,2048]{1,0:T(8,128)S(1)} %get-tuple-element.131, ...), kind=kLoop, calls=%fused_computation.12 | loop fusion | flops 10485760 | bytes 5242880 | tf_op jit(solution)/shard_map/convert
  37.9 0.0 copy-start
  37.9 0.0 copy-done.2
  37.9 0.0 copy-start.1
  37.9 1.4 %fusion.40 = (f32[32]{0:T(128)S(1)}, f32[32,16,50]{2,1,0:T(8,128)S(1)}) fusion(f32[32,50]{1,0:T(8,128)S(1)} %convolution_multiply_fusion, bf16[1,50,4096]{2,1,0:T(8,128)(2,1)S(1)} %copy-done.2, bf16[32,16,2048]{2,1,0:T(8,128)(2,1)S(1)} %get-tuple-element.128, bf16[32,16,2048]{2,1,0:T(8,128)(2,1)S(1)} %get-tuple-element.127, f32[32]{0:T(128)S(1)} %get-tuple-element.124), kind=kOutput, calls=%fused_computation.79 | convolution fusion | flops 218180576 | bytes 4712960 | tf_op jit(solution)/shard_map/while/body/eval_jaxpr/dot_general | solution.py:79
  39.3 0.5 exponential_reduce_fusion
  39.8 0.2 dynamic-update-slice.2
  40.1 0.2 dynamic-update-slice.3
  40.3 29.5 %all-reduce.5 = (f32[512]{0:T(512)S(1)}, f32[512]{0:T(512)S(1)}) all-reduce(f32[512]{0:T(512)S(1)} %dynamic-update-slice.2, f32[512]{0:T(512)S(1)} %dynamic-update-slice.3), channel_id=2, replica_groups=mesh['groups'=2,'blk'=4,'cls'=4] {'blk','cls'}, use_global_device_ids=true, to_apply=%add.2 | all-reduce | flops 1024 | bytes 8192
  69.8 0.1 slice.42
  69.8 0.1 slice.43
  69.9 0.1 reshape.391
  70.0 0.1 reshape.390
  70.1 0.6 while.2
  70.7 0.6 compare_select_fusion
  71.3 0.2 fusion.38
  71.4 0.3 fusion.20
  71.7 0.0 copy-done.1
  71.7 0.5 fusion.17
  72.3 2.6 %fusion.6 = f32[1,50,4096]{2,1,0:T(8,128)S(1)} fusion(bf16[32,16,2048]{2,1,0:T(8,128)(2,1)} %copy-done, bf16[32,16,2048]{2,1,0:T(8,128)(2,1)S(1)} %get-tuple-element.127, f32[50,2048]{1,0:T(8,128)S(1)} %fusion.17, f32[4096]{0:T(1024)S(1)} %pad_maximum_fusion.7, f32[32]{0:T(128)S(1)} %get-tuple-element.124, f32[32,16,50]{2,1,0:T(8,128)S(1)} %get-tuple-element.136, ...), kind=kOutput, calls=%fused_computation.9 | convolution fusion | flops 218846208 | bytes 5542400 | tf_op jit(solution)/shard_map/while/body/eval_jaxpr/dot_general | solution.py:105
  74.8 1.7 %copy.14 = f32[1,50,4096]{2,0,1:T(1,128)} copy(f32[1,50,4096]{2,1,0:T(8,128)S(1)} %fusion.6) | data formatting | bytes 1638400
  (40 shorter events, 0.5 us)
Async XLA Ops:
  0.6 23.8 %copy-start.5 = (u32[32]{0:T(128)S(1)}, u32[32]{0:T(128)}, u32[]{:S(2)}) copy-start(u32[32]{0:T(128)} %constant.123) | copy-start | bytes 388
  0.6 35.5 %copy-start.3 = (bf16[8,4096]{1,0:T(8,128)(2,1)S(1)}, bf16[8,4096]{1,0:T(8,128)(2,1)}, u32[]{:S(2)}) copy-start(bf16[8,4096]{1,0:T(8,128)(2,1)} %param.9) | copy-start | bytes 196612
  0.7 29.4 %copy-start.4 = (f32[2048]{0:T(1024)S(1)}, f32[2048]{0:T(1024)}, u32[]{:S(2)}) copy-start(f32[2048]{0:T(1024)} %param.12) | copy-start | bytes 24580
  0.7 23.3 %collective-permute-start = (bf16[8,4096]{1,0:T(8,128)(2,1)}, bf16[8,4096]{1,0:T(8,128)(2,1)S(1)}, u32[]{:S(2)}, u32[]{:S(2)}) collective-permute-start(bf16[8,4096]{1,0:T(8,128)(2,1)} %param.9), channel_id=1, source_target_pairs={{0,4},{4,8},{8,12},{12,0},{1,5},{5,9},{9,13},{13,1},{2,6},{6,10},{... | collective-permute-start | bytes 196616 | tf_op jit(solution)/shard_map/ppermute | solution.py:140
  24.0 6.1 %collective-permute-start.1 = (bf16[8,4096]{1,0:T(8,128)(2,1)S(1)}, bf16[8,4096]{1,0:T(8,128)(2,1)S(1)}, u32[]{:S(2)}, u32[]{:S(2)}) collective-permute-start(bf16[8,4096]{1,0:T(8,128)(2,1)S(1)} %collective-permute-done), channel_id=1, source_target_pairs={{0,4},{4,8},{8,12},{12,0},{1,5},{5,9},{9,13},{13,1},{2,6},{6,10},{... | collective-permute-start | bytes 196616 | tf_op jit(solution)/shard_map/ppermute | solution.py:140
  30.1 6.1 %collective-permute-start.2 = (bf16[8,4096]{1,0:T(8,128)(2,1)S(1)}, bf16[8,4096]{1,0:T(8,128)(2,1)S(1)}, u32[]{:S(2)}, u32[]{:S(2)}) collective-permute-start(bf16[8,4096]{1,0:T(8,128)(2,1)S(1)} %collective-permute-done.1), channel_id=1, source_target_pairs={{0,4},{4,8},{8,12},{12,0},{1,5},{5,9},{9,13},{13,1},{2,6},{6,10},{... | collective-permute-start | bytes 196616 | tf_op jit(solution)/shard_map/ppermute | solution.py:140
  36.3 1.6 %copy-start.2 = (bf16[1,50,4096]{2,1,0:T(8,128)(2,1)S(1)}, bf16[1,50,4096]{2,1,0:T(8,128)(2,1)}, u32[]{:S(2)}) copy-start(bf16[1,50,4096]{2,1,0:T(8,128)(2,1)} %param.10) | copy-start | bytes 1228804
  37.9 1.5 %copy-start = (bf16[32,16,2048]{2,1,0:T(8,128)(2,1)}, bf16[32,16,2048]{2,1,0:T(8,128)(2,1)S(1)}, u32[]{:S(2)}) copy-start(bf16[32,16,2048]{2,1,0:T(8,128)(2,1)S(1)} %get-tuple-element.128) | copy-start | bytes 6291460
  37.9 33.9 %copy-start.1 = (f32[16,2048]{1,0:T(8,128)S(1)}, f32[16,2048]{1,0:T(8,128)}, u32[]{:S(2)}) copy-start(f32[16,2048]{1,0:T(8,128)} %param.11) | copy-start | bytes 393220
